TPU v7x, 32 devices: a whole 2x2x4 slice. The times are simulated.
32 devices in a mesh: rep: 2 (over x), seq: 4 (over y, core), head: 4 (over z).
Axes of the slice: x: 2, y: 2, z: 4, core: 2. Of those that a mesh axis runs over, the one named last changes fastest.
Arguments:
- query_rows: bfloat16 [2048, 8192], P(('rep', 'seq'), 'head'), parts along dimension 0, may hold values from -128 to 128
- span_kv: bfloat16 [2, 2048, 1024], P(None, ('rep', 'seq'), 'head'), parts along dimension 1, may hold values from -6 to 6
- cache_kv: bfloat16 [2, 4096, 1024], P(None, ('rep', 'seq'), 'head'), parts along dimension 1, may hold values from -6 to 6
- cache_len: int32 [8], P(('rep', 'seq')), parts along dimension 0, may hold values from 1 to 512, 1024 in all
Outputs:
- attended: bfloat16 [2048, 8192], P(('rep', 'seq'), 'head'), parts along dimension 0
There are 2 independent parts, one for each index of `rep`. A program takes and returns all parts, laid end to end along the dimension named above; each array names one. Nothing has to cross between parts.
Inputs may be any that keep to these rules, and one draw needn't show every extreme that they name: `cache_len`: the earlier prompt is the filled slots of the instances in order; every instance has at least one filled slot and some instance is full.
All inputs are finite; a program needn't handle non-finite values. No bound on the sum of `cache_len` on one device may be relied on, other than what follows from the above.
Results may differ from a plain program's by a relative error of at most 0.007.
Values may be sent and summed in bfloat16 or wider, within the bound.
No kernel may reach another device: no remote copies, remote signals or barrier semaphores. Data moves between devices by JAX's collectives and lax.ppermute only.
A program may use at most 64 MiB of HBM per device.

v0:
```python
import jax
import jax.numpy as jnp
from jax import lax
from jax.sharding import PartitionSpec as P

HD = 128
blocked_tag = 1073741824
neg_value = -1e30


def fold_rows(carry_state, queries, positions, block_keys, block_values, block_tags):
    row_count = block_keys.shape[0]
    block_rows = 128
    block_count = row_count // block_rows
    kv_local = block_keys.shape[1] // HD
    key_blocks = block_keys.reshape(block_count, block_rows, kv_local, HD)
    value_blocks = block_values.reshape(block_count, block_rows, kv_local, HD)
    tag_blocks = block_tags.reshape(block_count, block_rows)

    def attend(carry_in, keys_in, values_in, tags_in):
        running_max, running_sum, running_out = carry_in
        scores = jnp.einsum(
            "qkgd,rkd->kgqr", queries, keys_in, preferred_element_type=jnp.float32
        ) * HD ** (-0.5)
        visible = tags_in[None, :] <= positions[:, None]
        scores = jnp.where(visible, scores, jnp.float32(neg_value))
        new_max = jnp.maximum(running_max, jnp.max(scores, axis=-1))
        rescale = jnp.exp(running_max - new_max)
        weights = jnp.where(visible, jnp.exp(scores - new_max[..., None]), jnp.float32(0.0))
        running_sum = running_sum * rescale + jnp.sum(weights, axis=-1)
        running_out = running_out * rescale[..., None] + jnp.einsum(
            "kgqr,rkd->kgqd",
            weights.astype(jnp.bfloat16),
            values_in,
            preferred_element_type=jnp.float32,
        )
        return (new_max, running_sum, running_out)

    def advance(carry_in, block_in):
        keys_in, values_in, tags_in = block_in
        carry_out = attend(carry_in, keys_in, values_in, tags_in)
        return (carry_out, None)

    carry_state, unused = lax.scan(advance, carry_state, (key_blocks, value_blocks, tag_blocks))
    return carry_state


def body(query_rows, span_kv, cache_kv, cache_len):
    tok_rows = query_rows.shape[0]
    kv_width = span_kv.shape[2]
    kv_local = kv_width // HD
    q_group = query_rows.shape[1] // kv_width
    own_index = lax.axis_index("seq")
    positions = own_index * tok_rows + jnp.arange(tok_rows, dtype=jnp.int32)
    queries = query_rows.reshape(tok_rows, kv_local, q_group, HD)
    slot_ids = jnp.arange(cache_kv.shape[1], dtype=jnp.int32)
    cache_tags = jnp.where(slot_ids < cache_len[0], jnp.int32(-1), jnp.int32(blocked_tag))
    carry_state = (
        jnp.full((kv_local, q_group, tok_rows), neg_value, jnp.float32),
        jnp.zeros((kv_local, q_group, tok_rows), jnp.float32),
        jnp.zeros((kv_local, q_group, tok_rows, HD), jnp.float32),
    )
    joined_keys = jnp.concatenate([cache_kv[0], span_kv[0]], axis=0)
    joined_values = jnp.concatenate([cache_kv[1], span_kv[1]], axis=0)
    joined_tags = jnp.concatenate([cache_tags, positions], axis=0)
    carry_state = fold_rows(
        carry_state,
        queries,
        positions,
        lax.all_gather(joined_keys, "seq", axis=0, tiled=True),
        lax.all_gather(joined_values, "seq", axis=0, tiled=True),
        lax.all_gather(joined_tags, "seq", axis=0, tiled=True),
    )
    running_max, running_sum, running_out = carry_state
    result = running_out / running_sum[..., None]
    result = jnp.transpose(result, (2, 0, 1, 3)).reshape(tok_rows, kv_local * q_group * HD)
    return result.astype(jnp.bfloat16)


def solution(mesh):
    in_specs = (
        P(("rep", "seq"), "head"),
        P(None, ("rep", "seq"), "head"),
        P(None, ("rep", "seq"), "head"),
        P(("rep", "seq")),
    )
    out_specs = P(("rep", "seq"), "head")
    return jax.shard_map(body, mesh=mesh, in_specs=in_specs, out_specs=out_specs, check_vma=False)
```

profile of v0, /device:TPU:0, one launch (start us, length us, event | category | flops | bytes accessed | tf_op | source)
XLA Modules:
  0.0 155.0 jit_solution(731224061644751360)
XLA Ops:
  6.5 1.1 slice_bitcast_fusion.2
  7.6 1.1 slice_bitcast_fusion
  8.7 0.8 pad_maximum_fusion.1
  9.5 0.8 pad_maximum_fusion
  11.1 1.3 copy.17
  12.4 1.6 %copy.20 = bf16[256,2,8,128]{3,0,2,1:T(8,128)(2,1)S(1)} copy(bf16[256,2,8,128]{0,3,2,1:T(8,128)(2,1)} %bitcast.62) | data formatting | bytes 2097152
  14.0 6.2 %all-gather = s32[4,1,768]{2,1,0:T(1,128)S(1)} all-gather(s32[1,1,768]{2,1,0:T(1,128)S(1)} %reshape.22), channel_id=1, replica_groups=mesh['rep'=2,'seq'=4,'head'=4] {'seq'}, dimensions={0}, use_global_device_ids=true | all-gather | bytes 15360 | tf_op jit(solution)/shard_map/all_gather | solution.py:72
  20.2 11.8 %all-gather.6.cloned.1.call-done = bf16[3072,256]{1,0:T(8,128)(2,1)} async-done(((bf16[768,256]{1,0:T(8,128)(2,1)}), bf16[3072,256]{1,0:T(8,128)(2,1)}) %all-gather.6.cloned.1.call-update) | async-done | bytes 1572880 | tf_op jit(solution)/shard_map/all_gather | solution.py:71
  32.0 3.5 %reshape.28 = bf16[24,128,2,128]{3,2,1,0:T(2,128)(2,1)} reshape(bf16[3072,256]{1,0:T(8,128)(2,1)} %all-gather.6.cloned.1.call-done) | data formatting | bytes 3145728 | tf_op jit(solution)/shard_map/reshape | solution.py:17
  35.5 17.7 %all-gather.4.cloned.1.call-done = bf16[3072,256]{1,0:T(8,128)(2,1)} async-done(((bf16[768,256]{1,0:T(8,128)(2,1)}), bf16[3072,256]{1,0:T(8,128)(2,1)}) %all-gather.4.cloned.1.call-update) | async-done | bytes 1572880 | tf_op jit(solution)/shard_map/all_gather | solution.py:70
  53.2 3.5 %reshape.27 = bf16[24,128,2,128]{3,2,1,0:T(2,128)(2,1)} reshape(bf16[3072,256]{1,0:T(8,128)(2,1)} %all-gather.4.cloned.1.call-done) | data formatting | bytes 3145728 | tf_op jit(solution)/shard_map/reshape | solution.py:16
  56.8 88.7 %while.15 = (s32[]{:T(128)}, f32[2,8,256]{2,1,0:T(8,128)S(1)}, f32[2,8,256]{2,1,0:T(8,128)S(1)}, f32[2,8,256,128]{3,2,1,0:T(8,128)S(1)}, s32[24,128]{1,0:T(8,128...) while((s32[]{:T(128)}, f32[2,8,256]{2,1,0:T(8,128)S(1)}, ...), condition=%wide.region_3.4_spmd.clone, body=%wide.region_0.3_spmd.clone.sunk | while | flops 276877568 | bytes 12324493 | solution.py:44
  56.9 1.0 constant_dynamic-slice_fusion.4
  58.9 1.5 fusion.34
  60.6 1.0 constant_dynamic-slice_fusion.4
  62.6 1.5 fusion.34
  64.3 1.0 constant_dynamic-slice_fusion.4
  65.7 0.5 fusion.32
  66.3 1.5 fusion.34
  68.0 1.0 constant_dynamic-slice_fusion.4
  70.0 1.5 fusion.34
  71.6 1.0 constant_dynamic-slice_fusion.4
  73.7 1.5 fusion.34
  75.3 1.0 constant_dynamic-slice_fusion.4
  77.4 1.5 fusion.34
  79.0 1.0 constant_dynamic-slice_fusion.4
  81.1 1.5 fusion.34
  82.7 1.0 constant_dynamic-slice_fusion.4
  84.8 1.5 fusion.34
  86.4 1.0 constant_dynamic-slice_fusion.4
  88.5 1.5 fusion.34
  90.1 1.0 constant_dynamic-slice_fusion.4
  92.2 1.5 fusion.34
  93.8 1.0 constant_dynamic-slice_fusion.4
  95.9 1.5 fusion.34
  97.5 1.0 constant_dynamic-slice_fusion.4
  99.5 1.5 fusion.34
  101.2 1.0 constant_dynamic-slice_fusion.4
  103.2 1.5 fusion.34
  104.9 1.0 constant_dynamic-slice_fusion.4
  106.9 1.5 fusion.34
  108.6 1.0 constant_dynamic-slice_fusion.4
  110.6 1.5 fusion.34
  112.3 1.0 constant_dynamic-slice_fusion.4
  114.3 1.5 fusion.34
  116.0 1.0 constant_dynamic-slice_fusion.4
  118.0 1.5 fusion.34
  119.7 1.0 constant_dynamic-slice_fusion.4
  121.7 1.5 fusion.34
  123.4 1.0 constant_dynamic-slice_fusion.4
  125.4 1.5 fusion.34
  127.1 1.0 constant_dynamic-slice_fusion.4
  129.1 1.5 fusion.34
  130.8 1.0 constant_dynamic-slice_fusion.4
  132.8 1.5 fusion.34
  134.5 1.0 constant_dynamic-slice_fusion.4
  136.5 1.5 fusion.34
  138.2 1.0 constant_dynamic-slice_fusion.4
  140.2 1.5 fusion.34
  141.9 1.0 constant_dynamic-slice_fusion.4
  143.9 1.5 fusion.34
  145.5 0.7 fusion.18
  146.2 0.7 copy.22
  146.9 1.2 copy.40
  (204 shorter events, 26.5 us)
Async XLA Ops:
  6.5 4.6 %copy-start = (bf16[256,2048]{1,0:T(8,128)(2,1)S(1)}, bf16[256,2048]{1,0:T(8,128)(2,1)}, u32[]{:S(2)}) copy-start(bf16[256,2048]{1,0:T(8,128)(2,1)} %param.6) | copy-start | bytes 3145732
  6.5 25.5 %all-gather.6.cloned.1.call-start = ((), (), s32[]{:S(2)}) async-start(), calls=%async_computation.1 | async-start | bytes 1966080 | tf_op jit(solution)/shard_map/all_gather | solution.py:71
  9.5 43.8 %all-gather.4.cloned.1.call-start = ((), (), s32[]{:S(2)}) async-start(), calls=%async_computation | async-start | bytes 1966080 | tf_op jit(solution)/shard_map/all_gather | solution.py:70
Sparse Core Ops, SparseCore 0:
  9.6 22.3 all-gather.5
  33.6 19.6 all-gather.3
where the time goes:
time: 156 us; the launch traced here: 155 us
  matrix products  47.6 us (31%)
  local copies, waits for them, and re-layouts  37.6 us (24%)
  waiting for transfers between devices  29.5 us (19%)
  other arithmetic  17.7 us (11%)
  between operations  14.2 us (9%)
  blocking collectives  6.19 us (4%)
  loops' own time  2.08 us (1%)
    dot_general x24, matrix products, attend(): jnp.einsum('kgqr,rkd->kgqd', weights.astype(jnp.bfloat16), values_in, pre...  36.4 us
    dynamic_slice x24, local copies, waits for them, and re-layouts, fold_rows(): lax.scan(advance, carry_state, (key_blocks, value_blocks, tag_blocks))  23.3 us
    all_gather x1, waiting for transfers between devices, body(): lax.all_gather(joined_keys, 'seq', axis=0, tiled=True)  17.7 us
    reduce_sum x24, other arithmetic, attend(): running_sum = running_sum * rescale + jnp.sum(weights, axis=-1)  12.7 us
    all_gather x1, waiting for transfers between devices, body(): lax.all_gather(joined_values, 'seq', axis=0, tiled=True)  11.8 us
    dot_general x24, matrix products, attend(): jnp.einsum('qkgd,rkd->kgqr', queries, keys_in, preferred_element_type=jnp...  11.2 us
    all_gather x1, blocking collectives, body(): lax.all_gather(joined_tags, 'seq', axis=0, tiled=True)  6.19 us
    unnamed x6, local copies, waits for them, and re-layouts  4.17 us
  transfers between devices with their start and end apart: 2, of which 2 were waited for; matrix products, arithmetic and copies ran while one was open for 5% of the time, Pallas kernels for 0%

commit v1 on v0

--- a/solution.py
+++ b/solution.py
@@ -2,6 +2,7 @@
 import jax.numpy as jnp
 from jax import lax
 from jax.sharding import PartitionSpec as P
+from jax.lax import axis_index, axis_size, ppermute
 
 HD = 128
 blocked_tag = 1073741824
@@ -63,11 +64,41 @@
     joined_keys = jnp.concatenate([cache_kv[0], span_kv[0]], axis=0)
     joined_values = jnp.concatenate([cache_kv[1], span_kv[1]], axis=0)
     joined_tags = jnp.concatenate([cache_tags, positions], axis=0)
+
+    def review_the_kinds(here_x, group_axis):
+        n_now = axis_size(group_axis)
+        pile = []
+        val, h_now, tmp = (n_now, axis_index(group_axis), here_x.shape[0])
+        u = 0
+        while u < val:
+            pile.append((u, (u + 1) % val))
+            u += 1
+        arrivals = []
+        u = 0
+        while u < val:
+            arrivals.append((u, (u - 1) % val))
+            u += 1
+        met_up = jnp.zeros((*here_x.shape[:0], val * tmp, *here_x.shape[1:]), here_x.dtype)
+        met_up = lax.dynamic_update_slice_in_dim(met_up, here_x, h_now * tmp, axis=0)
+        outcome_arr = val // 2
+        j = 1
+        b_now = clean = here_x
+        while j < outcome_arr + 1:
+            b_now = ppermute(b_now, perm=pile, axis_name=group_axis)
+            met_up = lax.dynamic_update_slice_in_dim(met_up, b_now, (h_now - j) % val * tmp, axis=0)
+            if j < val - outcome_arr:
+                clean = ppermute(clean, axis_name=group_axis, perm=arrivals)
+                met_up = lax.dynamic_update_slice_in_dim(
+                    met_up, clean, (h_now + j) % val * tmp, axis=0
+                )
+            j += 1
+        return met_up
+
     carry_state = fold_rows(
         carry_state,
         queries,
         positions,
-        lax.all_gather(joined_keys, "seq", axis=0, tiled=True),
+        review_the_kinds(joined_keys, "seq"),
         lax.all_gather(joined_values, "seq", axis=0, tiled=True),
         lax.all_gather(joined_tags, "seq", axis=0, tiled=True),
     )

time: 156 us -> 192 us (1.23); the launches traced: 155 us -> 189 us
  local copies, waits for them, and re-layouts: 37.6 us -> 67.3 us
  waiting for transfers between devices: 29.5 us -> 6.41 us
  matrix products: 47.6 us -> 67.9 us
  starting transfers between devices: 0.04 us -> 6.3 us
    dot_general x24, matrix products: 11.2 us -> 31.5 us  [attend(): jnp.einsum('qkgd,rkd->kgqr', queries, keys_in, preferred_element_type=jnp...]
    all_gather x1 -> x0, waiting for transfers between devices: 17.7 us -> none  [body(): lax.all_gather(joined_keys, 'seq', axis=0, tiled=True)]
    le x24, local copies, waits for them, and re-layouts: 0.22 us -> 16.5 us  [attend(): visible = tags_in[None, :] <= positions[:, None]]
    all_gather x1, waiting for transfers between devices: 11.8 us -> 0.01 us  [body(): lax.all_gather(joined_values, 'seq', axis=0, tiled=True)]
    unnamed x6 -> x10, local copies, waits for them, and re-layouts: 4.17 us -> 11.2 us
    ppermute x0 -> x3, waiting for transfers between devices: none -> 6.39 us  [the longest x2 6.39 us: review_the_kinds(): b_now = ppermute(b_now, perm=pile, axis_name=group_axis)]
    ppermute x0 -> x3, starting transfers between devices: none -> 6.29 us  [the longest x2 4.27 us: review_the_kinds(): b_now = ppermute(b_now, perm=pile, axis_name=group_axis)]
    dynamic_update_slice x0 -> x4, local copies, waits for them, and re-layouts: none -> 5.24 us  [the longest x2 2.61 us: review_the_kinds(): lax.dynamic_update_slice_in_dim(met_up, b_now, (h_now - j) % val * tmp, a...]
  transfers between devices with their start and end apart: 2 -> 4, of which waited for: 2 -> 1; matrix products, arithmetic and copies ran while one was open for 5% -> 12% of each run, Pallas kernels for 0% -> 0%
where the time goes in v1:
time: 192 us; the launch traced here: 189 us
  matrix products  67.9 us (35%)
  local copies, waits for them, and re-layouts  67.3 us (35%)
  other arithmetic  17.5 us (9%)
  between operations  14.1 us (7%)
  blocking collectives  7.5 us (4%)
  waiting for transfers between devices  6.41 us (3%)
  starting transfers between devices  6.3 us (3%)
    dot_general x24, matrix products, attend(): jnp.einsum('kgqr,rkd->kgqd', weights.astype(jnp.bfloat16), values_in, pre...  36.4 us
    dot_general x24, matrix products, attend(): jnp.einsum('qkgd,rkd->kgqr', queries, keys_in, preferred_element_type=jnp...  31.5 us
    dynamic_slice x24, local copies, waits for them, and re-layouts, fold_rows(): lax.scan(advance, carry_state, (key_blocks, value_blocks, tag_blocks))  21.4 us
    le x24, local copies, waits for them, and re-layouts, attend(): visible = tags_in[None, :] <= positions[:, None]  16.5 us
    reduce_sum x24, other arithmetic, attend(): running_sum = running_sum * rescale + jnp.sum(weights, axis=-1)  12.7 us
    unnamed x10, local copies, waits for them, and re-layouts  11.2 us
    all_gather x1, blocking collectives, body(): lax.all_gather(joined_tags, 'seq', axis=0, tiled=True)  7.5 us
    ppermute x2, waiting for transfers between devices, review_the_kinds(): b_now = ppermute(b_now, perm=pile, axis_name=group_axis)  6.39 us
  transfers between devices with their start and end apart: 4, of which 1 were waited for; matrix products, arithmetic and copies ran while one was open for 12% of the time, Pallas kernels for 0%

profile of v1, /device:TPU:0, one launch (start us, length us, event | category | flops | bytes accessed | tf_op | source)
XLA Modules:
  0.0 188.8 jit_solution(8410685243780598814)
XLA Ops:
  10.1 2.0 %collective-permute-start.1 = (bf16[768,256]{1,0:T(8,128)(2,1)S(1)}, bf16[768,256]{1,0:T(8,128)(2,1)}, u32[]{:S(2)}, u32[]{:S(2)}) collective-permute-start(bf16[768,256]{1,0:T(8,128)(2,1)S(1)} %pad_maximum_fusion), channel_id=1, source_target_pairs={{0,12},{4,0},{8,4},{12,8},{1,13},{5,1},{9,5},{13,9},{2,14},{6,2},{... | collective-permute-start | bytes 1179656 | tf_op jit(solution)/shard_map/ppermute | solution.py:90
  12.8 6.4 %collective-permute-done = bf16[768,256]{1,0:T(8,128)(2,1)} collective-permute-done((bf16[768,256]{1,0:T(8,128)(2,1)S(1)}, bf16[768,256]{1,0:T(8,128)(2,1)}, u32[]{:S(2)}, u32[]{:S(2)}) %collective-permute-start) | collective-permute-done | bytes 393248 | tf_op jit(solution)/shard_map/ppermute | solution.py:87
  19.1 3.8 %collective-permute-start.2 = (bf16[768,256]{1,0:T(8,128)(2,1)}, bf16[768,256]{1,0:T(8,128)(2,1)}, u32[]{:S(2)}, u32[]{:S(2)}) collective-permute-start(bf16[768,256]{1,0:T(8,128)(2,1)} %collective-permute-done), channel_id=1, source_target_pairs={{0,4},{4,8},{8,12},{12,0},{1,5},{5,9},{9,13},{13,1},{2,6},{6,10},{... | collective-permute-start | bytes 1179656 | tf_op jit(solution)/shard_map/ppermute | solution.py:87
  24.4 1.3 reshape.22
  25.7 1.3 copy.23
  27.0 1.6 copy.26
  28.7 7.5 %all-gather = s32[4,1,768]{2,1,0:T(1,128)} all-gather(s32[1,1,768]{2,1,0:T(1,128)} %reshape.22), channel_id=1, replica_groups=mesh['rep'=2,'seq'=4,'head'=4] {'seq'}, dimensions={0}, use_global_device_ids=true | all-gather | bytes 15360 | tf_op jit(solution)/shard_map/all_gather | solution.py:103
  36.2 1.3 broadcast_in_dim.42
  37.5 1.8 constant_dynamic-update-slice_fusion.3
  39.3 1.9 %copy.20 = bf16[768,256]{0,1:T(8,128)(2,1)} copy(bf16[768,256]{1,0:T(8,128)(2,1)} %collective-permute-done) | data formatting | bytes 786432 | tf_op jit(solution)/shard_map/ppermute | solution.py:87
  42.4 1.8 constant_dynamic-update-slice_fusion.2
  47.0 2.9 %copy.35 = bf16[32,8,24,128]{3,2,1,0:T(8,128)(2,1)} copy(bf16[32,8,24,128]{3,1,2,0:T(8,128)(2,1)} %bitcast.19) | data formatting | bytes 3145728
  49.9 2.9 %copy.25 = bf16[24,128,2,128]{3,1,2,0:T(8,128)(2,1)} copy(bf16[24,128,2,128]{1,0,3,2:T(8,128)(2,1)} %bitcast.66) | data formatting | bytes 3145728
  52.8 3.5 %reshape.27 = bf16[24,128,2,128]{3,2,1,0:T(2,128)(2,1)} reshape(bf16[3072,256]{1,0:T(8,128)(2,1)} %all-gather.3.cloned.1.call-done) | data formatting | bytes 3145728 | tf_op jit(solution)/shard_map/reshape | solution.py:18
  56.3 123.0 %while.15 = (s32[]{:T(128)}, f32[2,8,256]{2,1,0:T(8,128)S(1)}, f32[2,8,256]{2,1,0:T(8,128)S(1)}, f32[2,8,256,128]{3,2,1,0:T(8,128)S(1)}, s32[24,128]{1,0:T(8,128...) while((s32[]{:T(128)}, f32[2,8,256]{2,1,0:T(8,128)S(1)}, ...), condition=%wide.region_3.4_spmd.clone, body=%wide.region_0.3_spmd.clone.sunk | while | flops 276877568 | bytes 12193425 | solution.py:45
  57.9 1.3 fusion.34
  59.8 1.5 fusion.37
  63.1 1.3 fusion.34
  65.0 1.5 fusion.37
  68.2 1.3 fusion.34
  70.1 1.5 fusion.37
  73.3 1.3 fusion.34
  75.2 1.5 fusion.37
  78.5 1.3 fusion.34
  80.4 1.5 fusion.37
  83.6 1.3 fusion.34
  85.5 1.5 fusion.37
  88.7 1.3 fusion.34
  90.6 1.5 fusion.37
  93.8 1.3 fusion.34
  95.7 1.5 fusion.37
  99.0 1.3 fusion.34
  100.9 1.5 fusion.37
  104.1 1.3 fusion.34
  106.0 1.5 fusion.37
  109.2 1.3 fusion.34
  111.1 1.5 fusion.37
  114.4 1.3 fusion.34
  116.3 1.5 fusion.37
  119.5 1.3 fusion.34
  121.4 1.5 fusion.37
  124.6 1.3 fusion.34
  126.5 1.5 fusion.37
  129.7 1.3 fusion.34
  131.6 1.5 fusion.37
  134.9 1.3 fusion.34
  136.8 1.5 fusion.37
  140.0 1.3 fusion.34
  141.9 1.5 fusion.37
  145.1 1.3 fusion.34
  147.0 1.5 fusion.37
  150.2 1.3 fusion.34
  152.1 1.5 fusion.37
  155.4 1.3 fusion.34
  157.2 1.5 fusion.37
  160.5 1.3 fusion.34
  162.4 1.5 fusion.37
  165.6 1.3 fusion.34
  167.5 1.5 fusion.37
  170.7 1.3 fusion.34
  172.6 1.5 fusion.37
  175.8 1.3 fusion.34
  177.7 1.5 fusion.37
  180.7 1.2 copy.40
  (219 shorter events, 63.8 us)
Async XLA Ops:
  6.5 46.2 %all-gather.3.cloned.1.call-start = ((), (), s32[]{:S(2)}) async-start(), calls=%async_computation | async-start | bytes 1966080 | tf_op jit(solution)/shard_map/all_gather | solution.py:102
  7.5 18.2 %copy-start = (bf16[256,2048]{1,0:T(8,128)(2,1)S(1)}, bf16[256,2048]{1,0:T(8,128)(2,1)}, u32[]{:S(2)}) copy-start(bf16[256,2048]{1,0:T(8,128)(2,1)} %param.6) | copy-start | bytes 3145732
  9.6 9.6 %collective-permute-start = (bf16[768,256]{1,0:T(8,128)(2,1)S(1)}, bf16[768,256]{1,0:T(8,128)(2,1)}, u32[]{:S(2)}, u32[]{:S(2)}) collective-permute-start(bf16[768,256]{1,0:T(8,128)(2,1)S(1)} %pad_maximum_fusion), channel_id=1, source_target_pairs={{0,4},{4,8},{8,12},{12,0},{1,5},{5,9},{9,13},{13,1},{2,6},{6,10},{... | collective-permute-start | bytes 1179656 | tf_op jit(solution)/shard_map/ppermute | solution.py:87
  10.1 31.1 %collective-permute-start.1 = (bf16[768,256]{1,0:T(8,128)(2,1)S(1)}, bf16[768,256]{1,0:T(8,128)(2,1)}, u32[]{:S(2)}, u32[]{:S(2)}) collective-permute-start(bf16[768,256]{1,0:T(8,128)(2,1)S(1)} %pad_maximum_fusion), channel_id=1, source_target_pairs={{0,12},{4,0},{8,4},{12,8},{1,13},{5,1},{9,5},{13,9},{2,14},{6,2},{... | collective-permute-start | bytes 1179656 | tf_op jit(solution)/shard_map/ppermute | solution.py:90
  19.1 25.9 %collective-permute-start.2 = (bf16[768,256]{1,0:T(8,128)(2,1)}, bf16[768,256]{1,0:T(8,128)(2,1)}, u32[]{:S(2)}, u32[]{:S(2)}) collective-permute-start(bf16[768,256]{1,0:T(8,128)(2,1)} %collective-permute-done), channel_id=1, source_target_pairs={{0,4},{4,8},{8,12},{12,0},{1,5},{5,9},{9,13},{13,1},{2,6},{6,10},{... | collective-permute-start | bytes 1179656 | tf_op jit(solution)/shard_map/ppermute | solution.py:87
  52.7 3.5 %copy-start.1 = (f32[2,8,256]{2,1,0:T(8,128)S(1)}, f32[2,8,256]{2,1,0:T(8,128)}, u32[]{:S(2)}) copy-start(f32[2,8,256]{2,1,0:T(8,128)} %custom-call.1) | copy-start | bytes 49156
Sparse Core Ops, SparseCore 0:
  9.6 26.5 all-gather.2
